TPU v7x, 256 devices: a whole 4x4x8 slice. The times are simulated.
256 devices in a mesh: section: 2 (over core), tok: 32 (over z, y), rep: 4 (over x).
Axes of the slice: x: 4, y: 4, z: 8, core: 2. Of those that a mesh axis runs over, the one named last changes fastest.
Arguments:
- inputs: bfloat16 [2, 4096, 1024], P(None, 'tok')
- segment_ids: int32 [2, 4096], replicated, may hold values from 0 to 7, as said below
- picks: int32 [2, 4096, 2], P(None, 'tok'), may hold values from 0 to 15, all different within a row; in each aligned block of 128 rows (0 to 127, 128 to 255, ..., all dimensions but the last counted through in order) at most 20 rows name the same one
- page_table: int32 [2, 32], replicated, may hold values from 0 to 31, each once within a row
- norm_gains: float32 [2, 2, 1024], P('section'), may hold values from 0.1 to 1.9
- attn_qkv: bfloat16 [2, 1024, 3, 1024], P('section', None, None, 'rep')
- attn_out: bfloat16 [2, 1024, 1024], P('section', 'rep'), may hold values from -0.1875 to 0.1875
- router: bfloat16 [2, 1024, 16], P('section')
- expert_in: bfloat16 [2, 32, 1024, 2, 1408], P('section', 'tok', None, None, 'rep'), may hold values from -0.1875 to 0.1875
- expert_out: bfloat16 [2, 32, 1408, 1024], P('section', 'tok', 'rep')
Outputs:
- layer_out: bfloat16 [2, 2, 4096, 1024], P('section', None, 'tok')
- kv_pages: bfloat16 [2, 2, 32, 128, 2, 1024], P('section', None, 'tok', None, None, 'rep')
Inputs may be any that keep to these rules, and one draw needn't show every extreme that they name: `picks`: within the tokens of one index of tok in one micro-batch, at most 20 tokens pick one expert, and some expert is picked by exactly 20. `segment_ids`: ids never fall along a micro-batch; every prompt has at least one token, a prompt spans at most 2048 tokens and one spans exactly 2048. `page_table`: each row is a permutation.
All inputs are finite; a program needn't handle non-finite values.
Results may differ from a plain program's by a relative error of at most 0.034.
Values may be sent and summed in bfloat16 or wider, within the bound.
No kernel may reach another device: no remote copies, remote signals or barrier semaphores. Data moves between devices by JAX's collectives and lax.ppermute only.
A program may use at most 128 MiB of HBM per device.

v0:
```python
import jax
import jax.numpy as jnp
from jax import lax
from jax.sharding import PartitionSpec as P

HEAD_DIM = 64
TOP = 2
PAGE = 128
CAP = 20
NEG_FILL = -1e30


def shifted(value, axis, steps):
    count = lax.axis_size(axis)
    first, last = (max(0, -steps), min(count, count - steps))
    return lax.ppermute(value, axis, [(source, source + steps) for source in range(first, last)])


def rms_scale(values, gains):
    return values * lax.rsqrt(jnp.mean(values * values, axis=-1, keepdims=True) + 1e-06) * gains


def attend(carry, queries, keys_vals, seg_query, pos_query, seg_key, pos_key):
    run_max, run_sum, run_acc = carry
    heads_here = run_acc.shape[0]
    head_size = run_acc.shape[2]
    rows_key = keys_vals.shape[0]
    key_part = keys_vals[:, 0].reshape(rows_key, heads_here, head_size)
    val_part = keys_vals[:, 1].reshape(rows_key, heads_here, head_size).astype(jnp.float32)
    scores = jnp.einsum(
        "thd,nhd->htn", queries, key_part, preferred_element_type=jnp.float32
    ) * head_size ** (-0.5)
    visible = (seg_query[:, None] == seg_key[None, :]) & (pos_query[:, None] >= pos_key[None, :])
    masked = jnp.where(visible[None], scores, NEG_FILL)
    new_max = jnp.maximum(run_max, jnp.max(masked, axis=-1))
    weights = jnp.where(visible[None], jnp.exp(masked - new_max[..., None]), 0.0)
    decay = jnp.exp(run_max - new_max)
    run_sum = run_sum * decay + jnp.sum(weights, axis=-1)
    run_acc = run_acc * decay[..., None] + jnp.einsum(
        "htn,nhd->htd", weights, val_part, precision=lax.Precision.HIGHEST
    )
    return (new_max, run_sum, run_acc)


def place_pages(pages, keys_vals, table_row, tok_index):
    rows_here = keys_vals.shape[0]
    blocks_dev = pages.shape[0]
    page_rows = pages.shape[1]
    block_ids = jnp.arange(table_row.shape[0], dtype=jnp.int32)
    wanted = tok_index * blocks_dev + 0
    source = jnp.sum(jnp.where(table_row == wanted, block_ids, 0))
    offset = source * page_rows
    inside = (offset >= 0) & (offset + page_rows <= rows_here)
    block = lax.dynamic_slice_in_dim(
        keys_vals, jnp.clip(offset, 0, rows_here - page_rows), page_rows, 0
    )
    updated = [jnp.where(inside, block, pages[0])]
    return jnp.stack(updated)


def one_layer(layer_in, seg_all, table_row, pick_rows, gains, w_qkv, w_out, w_router, w_in, w_down):
    tok_index = lax.axis_index("tok")
    tok_count = lax.axis_size("tok")
    tok_rows = layer_in.shape[0]
    width = layer_in.shape[1]
    col_width = w_qkv.shape[1] // 3
    head_count = col_width // HEAD_DIM
    experts_all = w_router.shape[1]
    local_pieces = w_in.shape[0]
    split_count = local_pieces * tok_count // experts_all
    blocks_dev = tok_rows // PAGE
    row_ids = jnp.arange(tok_rows, dtype=jnp.int32)
    pos_query = tok_index * tok_rows + row_ids
    seg_query = lax.dynamic_slice_in_dim(seg_all, tok_index * tok_rows, tok_rows)
    resid = layer_in.astype(jnp.float32)
    normed = rms_scale(resid, gains[0]).astype(jnp.bfloat16)
    projected = jnp.dot(normed, w_qkv, preferred_element_type=jnp.float32).astype(jnp.bfloat16)
    projected = projected.reshape(tok_rows, 3, col_width)
    queries = projected[:, 0].reshape(tok_rows, head_count, HEAD_DIM)
    keys_vals = projected[:, 1:]
    soft_init = (
        jnp.full((head_count, tok_rows), NEG_FILL, jnp.float32),
        jnp.zeros((head_count, tok_rows), jnp.float32),
        jnp.zeros((head_count, tok_rows, HEAD_DIM), jnp.float32),
    )
    empty_pages = jnp.zeros((blocks_dev, PAGE, 2, col_width), jnp.bfloat16)
    piece = lax.all_gather(keys_vals, "tok", axis=0, tiled=True)
    rows_key = piece.shape[0]
    step_rows = 1024
    while rows_key % step_rows != 0:
        step_rows = step_rows // 2
    turns = rows_key // step_rows

    def key_block(index, soft_now):
        start = index * step_rows
        block = lax.dynamic_slice_in_dim(piece, start, step_rows, 0)
        seg_key = lax.dynamic_slice_in_dim(seg_all, start, step_rows)
        pos_key = start + jnp.arange(step_rows, dtype=jnp.int32)
        return attend(soft_now, queries, block, seg_query, pos_query, seg_key, pos_key)

    soft_next = lax.fori_loop(0, turns, key_block, soft_init)
    pages = place_pages(empty_pages, piece, table_row, tok_index)
    run_max, run_sum, run_acc = soft_next
    context = (
        (run_acc / run_sum[..., None])
        .transpose(1, 0, 2)
        .reshape(tok_rows, col_width)
        .astype(jnp.bfloat16)
    )
    attn_part = jnp.dot(context, w_out, preferred_element_type=jnp.float32)
    mid = resid + lax.psum(attn_part, "rep")
    normed_mid = rms_scale(mid, gains[1]).astype(jnp.bfloat16)
    logits = jnp.dot(normed_mid, w_router, preferred_element_type=jnp.float32)
    expert_ids = jnp.arange(experts_all, dtype=jnp.int32)
    chosen = (pick_rows[:, :, None] == expert_ids[None, None, :]).astype(jnp.int32)
    picked_logit = jnp.sum(chosen.astype(jnp.float32) * logits[:, None, :], axis=-1)
    top_logit = jnp.max(picked_logit, axis=-1, keepdims=True)
    raised = jnp.exp(picked_logit - top_logit)
    gate_vals = raised / jnp.sum(raised, axis=-1, keepdims=True)
    ordered = chosen.transpose(1, 0, 2).reshape(TOP * tok_rows, experts_all)
    slot_of = jnp.sum((jnp.cumsum(ordered, axis=0) - 1) * ordered, axis=-1)
    flat_slot = pick_rows.T.reshape(TOP * tok_rows) * CAP + slot_of
    slot_ids = jnp.arange(experts_all * CAP, dtype=jnp.int32)
    hits = (flat_slot[:, None] == slot_ids[None, :]).astype(jnp.int32)
    hits = jnp.sum(hits.reshape(TOP, tok_rows, experts_all * CAP), axis=0).astype(jnp.bfloat16)
    dispatch = lax.dot_general(
        hits, normed_mid, (((0,), (0,)), ((), ())), preferred_element_type=jnp.float32
    ).astype(jnp.bfloat16)
    copies = jnp.broadcast_to(
        dispatch.reshape(experts_all, 1, CAP, width), (experts_all, split_count, CAP, width)
    )
    copies = copies.reshape(tok_count, local_pieces, CAP, width)
    act = jnp.einsum(
        "secd,edgf->secgf",
        lax.all_to_all(copies, "tok", split_axis=0, concat_axis=0, tiled=True),
        w_in,
        preferred_element_type=jnp.float32,
    )
    hidden = (jax.nn.gelu(act[..., 0, :]) * act[..., 1, :]).astype(jnp.bfloat16)
    returned = lax.all_to_all(
        jnp.einsum("secf,efd->secd", hidden, w_down, preferred_element_type=jnp.float32).astype(
            jnp.bfloat16
        ),
        "tok",
        split_axis=0,
        concat_axis=0,
        tiled=True,
    )
    summed = jnp.sum(
        returned.reshape(experts_all, split_count, CAP, width).astype(jnp.float32), axis=1
    )
    summed = summed.reshape(experts_all * CAP, width)
    gathered = jnp.take(summed, flat_slot, axis=0).reshape(TOP, tok_rows, width)
    expert_local = jnp.sum(gate_vals.T[:, :, None] * gathered, axis=0)
    expert_total = lax.psum(expert_local, "rep")
    layer_result = (mid + expert_total).astype(jnp.bfloat16)
    return (layer_result, pages)


def per_device(
    inputs,
    segment_ids,
    picks,
    page_table,
    norm_gains,
    attn_qkv,
    attn_out,
    router,
    expert_in,
    expert_out,
):
    section_index = lax.axis_index("section")
    is_first = section_index == 0
    width = inputs.shape[2]
    own = (
        norm_gains[0],
        attn_qkv[0].reshape(width, -1),
        attn_out[0],
        router[0],
        expert_in[0],
        expert_out[0],
    )
    swap = [(0, 1), (1, 0)]
    other = tuple((lax.ppermute(w, "section", swap) for w in own))
    weights_of = [
        tuple((jnp.where(is_first, a, b) for a, b in zip(own, other))),
        tuple((jnp.where(is_first, b, a) for a, b in zip(own, other))),
    ]
    micro = section_index
    hidden = lax.dynamic_index_in_dim(inputs, micro, 0, keepdims=False)
    seg_all = lax.dynamic_index_in_dim(segment_ids, micro, 0, keepdims=False)
    table_row = lax.dynamic_index_in_dim(page_table, micro, 0, keepdims=False)
    pick_rows = lax.dynamic_index_in_dim(picks, micro, 0, keepdims=False)
    results = []
    for layer in range(2):
        hidden, pages = one_layer(hidden, seg_all, table_row, pick_rows, *weights_of[layer])
        results.append((hidden, pages))
    (res0, pages0), (res1, pages1) = results
    got0 = lax.ppermute(res0, "section", [(1, 0)])
    gotp0 = lax.ppermute(pages0, "section", [(1, 0)])
    got1 = lax.ppermute(res1, "section", [(0, 1)])
    gotp1 = lax.ppermute(pages1, "section", [(0, 1)])
    outputs = jnp.where(is_first, jnp.stack([res0, got0]), jnp.stack([got1, res1]))
    page_out = jnp.where(is_first, jnp.stack([pages0, gotp0]), jnp.stack([gotp1, pages1]))
    return (outputs[None], page_out[None])


def solution(mesh):
    return jax.shard_map(
        per_device,
        mesh=mesh,
        in_specs=(
            P(None, "tok", None),
            P(),
            P(None, "tok", None),
            P(),
            P("section", None, None),
            P("section", None, None, "rep"),
            P("section", "rep", None),
            P("section", None, None),
            P("section", "tok", None, None, "rep"),
            P("section", "tok", "rep", None),
        ),
        out_specs=(P("section", None, "tok", None), P("section", None, "tok", None, None, "rep")),
        check_vma=False,
    )
```

profile of v0, /device:TPU:1, one launch (start us, length us, event | category | flops | bytes accessed | tf_op | source)
XLA Modules:
  0.0 634.5 jit_solution(9774270104577038417)
XLA Ops:
  7.2 1.8 copy.55
  9.0 3.3 collective-permute-start.1
  12.6 2.9 collective-permute-done
  15.5 2.1 fusion.48
  19.5 79.9 %all-gather.3.cloned.1.call-done = bf16[4096,2,256]{0,2,1:T(8,128)(2,1)} async-done(((bf16[128,2,256]{0,2,1:T(8,128)(2,1)}), bf16[4096,2,256]{0,2,1:T(8,128)(2,1)}) %all-gather.3.cloned.1.call-update) | async-done | bytes 4194320 | tf_op jit(solution)/shard_map/all_gather | solution.py:87
  99.4 17.1 %while.36 = (s32[]{:T(128)}, f32[4,128]{1,0:T(4,128)S(1)}, f32[4,128]{1,0:T(4,128)S(1)}, f32[4,128,64]{1,2,0:T(8,128)S(1)}, s32[128]{0:T(128)S(1)}, /*index=5*/s...) while((s32[]{:T(128)}, f32[4,128]{1,0:T(4,128)S(1)}, ...), condition=%wide.region_4.5_spmd.clone, body=%wide.region_1.4_spmd.clone.sunk | while | flops 476548736 | bytes 10344167 | solution.py:101
  102.2 1.4 fusion.180
  106.5 1.4 fusion.180
  118.0 49.1 %all-reduce.5.cloned.1.call-done = f32[128,1024]{1,0:T(8,128)} async-done(((f32[128,1024]{1,0:T(8,128)}), f32[128,1024]{1,0:T(8,128)}) %all-reduce.5.cloned.1.call-update) | async-done | bytes 524304 | tf_op jit(solution)/shard_map/psum | solution.py:111
  170.0 1.4 broadcast_in_dim.165
  171.5 9.7 %all-to-all-start = ((bf16[32,1,20,1024]{3,2,1,0:T(8,128)(2,1)}), bf16[32,1,20,1024]{3,2,1,0:T(8,128)(2,1)S(1)}, u32[]{:S(2)}, u32[]{:S(2)}) async-start(bf16[32,1,20,1024]{3,2,1,0:T(8,128)(2,1)} %bitcast.29), calls=%async_computation | async-start | bytes 3145728 | tf_op jit(solution)/shard_map/all_to_all | solution.py:135
  181.2 3.2 collective-permute-start.5
  184.7 2.9 collective-permute-done.5
  187.6 28.6 %all-to-all-done = bf16[32,1,20,1024]{3,2,1,0:T(8,128)(2,1)S(1)} async-done(((bf16[32,1,20,1024]{3,2,1,0:T(8,128)(2,1)}), bf16[32,1,20,1024]{3,2,1,0:T(8,128)(2,1)S(1)}, u32[]{:S(2)}, u32[]{:S(2)}) %all-to-all-start) | async-done | bytes 1310752 | tf_op jit(solution)/shard_map/all_to_all | solution.py:135
  216.2 3.6 convolution_bitcast_fusion.1
  219.8 2.3 fusion.42
  222.1 2.0 copy.59
  224.1 7.5 %all-to-all-start.1 = ((bf16[32,1,20,1024]{3,2,1,0:T(8,128)(2,1)}), bf16[32,1,20,1024]{3,2,1,0:T(8,128)(2,1)S(1)}, u32[]{:S(2)}, u32[]{:S(2)}) async-start(bf16[32,1,20,1024]{3,2,1,0:T(8,128)(2,1)} %copy.59), calls=%async_computation.1 | async-start | bytes 3145728 | tf_op jit(solution)/shard_map/all_to_all | solution.py:140
  231.7 2.9 collective-permute-start.3
  235.6 31.5 %all-to-all-done.1 = bf16[32,1,20,1024]{3,2,1,0:T(8,128)(2,1)S(1)} async-done(((bf16[32,1,20,1024]{3,2,1,0:T(8,128)(2,1)}), bf16[32,1,20,1024]{3,2,1,0:T(8,128)(2,1)S(1)}, u32[]{:S(2)}, u32[]{:S(2)}) %all-to-all-start.1) | async-done | bytes 1310752 | tf_op jit(solution)/shard_map/all_to_all | solution.py:140
  269.9 47.1 %all-reduce.7.cloned.1.call-done = f32[128,1024]{1,0:T(8,128)} async-done(((f32[128,1024]{1,0:T(8,128)}), f32[128,1024]{1,0:T(8,128)}) %all-reduce.7.cloned.1.call-update) | async-done | bytes 524304 | tf_op jit(solution)/shard_map/psum | solution.py:155
  319.9 84.1 %all-gather.5.cloned.1.call-done = bf16[4096,2,256]{0,2,1:T(8,128)(2,1)} async-done(((bf16[128,2,256]{0,2,1:T(8,128)(2,1)}), bf16[4096,2,256]{0,2,1:T(8,128)(2,1)}) %all-gather.5.cloned.1.call-update) | async-done | bytes 4194320 | tf_op jit(solution)/shard_map/all_gather | solution.py:87
  404.0 17.1 %while.37 = (s32[]{:T(128)}, f32[4,128]{1,0:T(4,128)S(1)}, f32[4,128]{1,0:T(4,128)S(1)}, f32[4,128,64]{1,2,0:T(8,128)S(1)}, s32[128]{0:T(128)S(1)}, /*index=5*/s...) while((s32[]{:T(128)}, f32[4,128]{1,0:T(4,128)S(1)}, ...), condition=%wide.region_21.23_spmd.clone, body=%wide.region_18.22_spmd.clone.sunk | while | flops 476548736 | bytes 10344167 | solution.py:101
  422.3 49.5 %all-reduce.9.cloned.1.call-done = f32[128,1024]{1,0:T(8,128)} async-done(((f32[128,1024]{1,0:T(8,128)}), f32[128,1024]{1,0:T(8,128)}) %all-reduce.9.cloned.1.call-update) | async-done | bytes 524304 | tf_op jit(solution)/shard_map/psum | solution.py:111
  474.8 45.7 %all_to_all.20 = bf16[32,1,20,1024]{3,2,1,0:T(8,128)(2,1)S(1)} all-to-all(bf16[32,1,20,1024]{3,2,1,0:T(8,128)(2,1)S(1)} %bitcast.258), channel_id=1, replica_groups=mesh['section'=2,'tok'=32,'rep'=4] {'tok'}, dimensions={0} | all-to-all | bytes 2621440 | tf_op jit(solution)/shard_map/all_to_all | solution.py:135
  520.5 1.8 convolution_bitcast_fusion
  523.4 2.0 copy.64
  525.3 6.1 all-to-all-start.3
  531.7 31.8 %all-to-all-done.3 = bf16[32,1,20,1024]{3,2,1,0:T(8,128)(2,1)S(1)} async-done(((bf16[32,1,20,1024]{3,2,1,0:T(8,128)(2,1)}), bf16[32,1,20,1024]{3,2,1,0:T(8,128)(2,1)S(1)}, u32[]{:S(2)}, u32[]{:S(2)}) %all-to-all-start.3) | async-done | bytes 1310752 | tf_op jit(solution)/shard_map/all_to_all | solution.py:140
  568.6 9.9 %collective-permute-start.8 = (bf16[1,128,2,256]{1,3,2,0:T(8,128)(2,1)S(1)}, bf16[1,128,2,256]{1,3,2,0:T(8,128)(2,1)S(1)}, u32[]{:S(2)}, u32[]{:S(2)}) collective-permute-start(bf16[1,128,2,256]{1,3,2,0:T(8,128)(2,1)S(1)} %get-tuple-element.462), channel_id=1, source_target_pairs={{128,0},{129,1},{130,2},{131,3},{132,4},{133,5},{134,6},{135,7},{1... | collective-permute-start | bytes 393224 | tf_op jit(solution)/shard_map/ppermute | solution.py:200
  579.8 37.5 %all-reduce.11.cloned.1.call-done = f32[128,1024]{1,0:T(8,128)} async-done(((f32[128,1024]{1,0:T(8,128)}), f32[128,1024]{1,0:T(8,128)}) %all-reduce.11.cloned.1.call-update) | async-done | bytes 524304 | tf_op jit(solution)/shard_map/psum | solution.py:155
  622.1 3.7 collective-permute-done.9
  (224 shorter events, 61.9 us)
Async XLA Ops:
  7.2 12.2 %copy-start = (s32[2,4096]{1,0:T(2,128)S(1)}, s32[2,4096]{1,0:T(2,128)}, u32[]{:S(2)}) copy-start(s32[2,4096]{1,0:T(2,128)} %param.17) | copy-start | bytes 98308
  7.2 92.2 %all-gather.3.cloned.1.call-start = ((), (), s32[]{:S(2)}) async-start(), calls=%async_computation.4 | async-start | bytes 4325376 | tf_op jit(solution)/shard_map/all_gather | solution.py:87
  9.0 8.7 %copy-start.10 = (bf16[1,1024,3,256]{1,3,2,0:T(8,128)(2,1)}, bf16[1,1024,3,256]{1,3,2,0:T(8,128)(2,1)S(1)}, u32[]{:S(2)}) copy-start(bf16[1,1024,3,256]{1,3,2,0:T(8,128)(2,1)S(1)} %copy.55) | copy-start | bytes 4718596
  9.0 6.5 %collective-permute-start.1 = (bf16[1024,768]{0,1:T(8,128)(2,1)S(1)}, bf16[1024,768]{0,1:T(8,128)(2,1)}, u32[]{:S(2)}, u32[]{:S(2)}) collective-permute-start(bf16[1024,768]{0,1:T(8,128)(2,1)S(1)} %bitcast.264), channel_id=1, source_target_pairs={{0,128},{128,0},{1,129},{129,1},{2,130},{130,2},{3,131},{131,3},{4... | collective-permute-start | bytes 4718600 | tf_op jit(solution)/shard_map/ppermute | solution.py:184
  12.3 3.2 collective-permute-start
  18.6 148.6 %all-reduce.5.cloned.1.call-start = ((), (), s32[]{:S(2)}) async-start(), calls=%async_computation.5 | async-start | bytes 1048576 | tf_op jit(solution)/shard_map/psum | solution.py:111
  18.6 97.9 %collective-permute-start.2 = (bf16[256,1024]{1,0:T(8,128)(2,1)S(1)}, bf16[256,1024]{1,0:T(8,128)(2,1)S(1)}, u32[]{:S(2)}, u32[]{:S(2)}) collective-permute-start(bf16[256,1024]{1,0:T(8,128)(2,1)S(1)} %bitcast.263), channel_id=1, source_target_pairs={{0,128},{128,0},{1,129},{129,1},{2,130},{130,2},{3,131},{131,3},{4... | collective-permute-start | bytes 1572872 | tf_op jit(solution)/shard_map/ppermute | solution.py:184
  116.6 51.8 %copy-start.8 = (bf16[256,1024]{1,0:T(8,128)(2,1)}, bf16[256,1024]{1,0:T(8,128)(2,1)S(1)}, u32[]{:S(2)}) copy-start(bf16[256,1024]{1,0:T(8,128)(2,1)S(1)} %collective-permute-done.2) | copy-start | bytes 1572868
  171.5 13.0 %copy-start.17 = (bf16[1,1,352,1024]{3,2,1,0:T(8,128)(2,1)S(1)}, bf16[1,1,352,1024]{3,2,1,0:T(8,128)(2,1)}, u32[]{:S(2)}) copy-start(bf16[1,1,352,1024]{3,2,1,0:T(8,128)(2,1)} %param.25) | copy-start | bytes 2162692
  171.5 44.8 %all-to-all-start = ((bf16[32,1,20,1024]{3,2,1,0:T(8,128)(2,1)}), bf16[32,1,20,1024]{3,2,1,0:T(8,128)(2,1)S(1)}, u32[]{:S(2)}, u32[]{:S(2)}) async-start(bf16[32,1,20,1024]{3,2,1,0:T(8,128)(2,1)} %bitcast.29), calls=%async_computation | async-start | bytes 3145728 | tf_op jit(solution)/shard_map/all_to_all | solution.py:135
  181.2 6.4 %collective-permute-start.5 = (bf16[1,1024,2,352]{1,3,2,0:T(8,128)(2,1)}, bf16[1,1024,2,352]{1,3,2,0:T(8,128)(2,1)}, u32[]{:S(2)}, u32[]{:S(2)}) collective-permute-start(bf16[1,1024,2,352]{1,3,2,0:T(8,128)(2,1)} %bitcast.285), channel_id=1, source_target_pairs={{0,128},{128,0},{1,129},{129,1},{2,130},{130,2},{3,131},{131,3},{4... | collective-permute-start | bytes 4325384 | tf_op jit(solution)/shard_map/ppermute | solution.py:184
  184.4 35.4 %collective-permute-start.4 = (bf16[1,352,1024]{2,1,0:T(8,128)(2,1)S(1)}, bf16[1,352,1024]{2,1,0:T(8,128)(2,1)}, u32[]{:S(2)}, u32[]{:S(2)}) collective-permute-start(bf16[1,352,1024]{2,1,0:T(8,128)(2,1)S(1)} %bitcast.286), channel_id=1, source_target_pairs={{0,128},{128,0},{1,129},{129,1},{2,130},{130,2},{3,131},{131,3},{4... | collective-permute-start | bytes 2162696 | tf_op jit(solution)/shard_map/ppermute | solution.py:184
  224.1 7.6 %copy-start.12 = (bf16[1,1024,16]{1,2,0:T(8,128)(2,1)S(1)}, bf16[1,1024,16]{1,2,0:T(8,128)(2,1)}, u32[]{:S(2)}) copy-start(bf16[1,1024,16]{1,2,0:T(8,128)(2,1)} %param.23) | copy-start | bytes 98308
  224.1 43.1 %all-to-all-start.1 = ((bf16[32,1,20,1024]{3,2,1,0:T(8,128)(2,1)}), bf16[32,1,20,1024]{3,2,1,0:T(8,128)(2,1)S(1)}, u32[]{:S(2)}, u32[]{:S(2)}) async-start(bf16[32,1,20,1024]{3,2,1,0:T(8,128)(2,1)} %copy.59), calls=%async_computation.1 | async-start | bytes 3145728 | tf_op jit(solution)/shard_map/all_to_all | solution.py:140
  231.6 85.4 %all-reduce.7.cloned.1.call-start = ((), (), s32[]{:S(2)}) async-start(), calls=%async_computation.6 | async-start | bytes 1048576 | tf_op jit(solution)/shard_map/psum | solution.py:155
  231.7 3.7 collective-permute-start.3
  268.7 48.3 %copy-start.3 = (f32[128,1024]{1,0:T(8,128)S(1)}, f32[128,1024]{1,0:T(8,128)}, u32[]{:S(2)}) copy-start(f32[128,1024]{1,0:T(8,128)} %all-reduce.5.cloned.1.call-done) | copy-start | bytes 1572868
  268.8 48.3 %copy-start.5 = (bf16[2,128,1024]{2,1,0:T(8,128)(2,1)S(1)}, bf16[2,128,1024]{2,1,0:T(8,128)(2,1)}, u32[]{:S(2)}) copy-start(bf16[2,128,1024]{2,1,0:T(8,128)(2,1)} %param.16) | copy-start | bytes 1572868
  268.9 49.3 %copy-start.11 = (bf16[1,1024,3,256]{1,3,2,0:T(8,128)(2,1)S(1)}, bf16[1,1024,3,256]{1,3,2,0:T(8,128)(2,1)}, u32[]{:S(2)}) copy-start(bf16[1,1024,3,256]{1,3,2,0:T(8,128)(2,1)} %copy-done.10) | copy-start | bytes 4718596
  269.9 134.2 %all-gather.5.cloned.1.call-start = ((), (), s32[]{:S(2)}) async-start(), calls=%async_computation.7 | async-start | bytes 4325376 | tf_op jit(solution)/shard_map/all_gather | solution.py:87
  319.8 152.0 %all-reduce.9.cloned.1.call-start = ((), (), s32[]{:S(2)}) async-start(), calls=%async_computation.8 | async-start | bytes 1048576 | tf_op jit(solution)/shard_map/psum | solution.py:111
  404.0 17.2 %copy-start.7 = (bf16[1,256,1024]{2,1,0:T(8,128)(2,1)S(1)}, bf16[1,256,1024]{2,1,0:T(8,128)(2,1)}, u32[]{:S(2)}) copy-start(bf16[1,256,1024]{2,1,0:T(8,128)(2,1)} %param.22) | copy-start | bytes 1572868
  404.0 17.2 %copy-start.9 = (bf16[256,1024]{1,0:T(8,128)(2,1)S(1)}, bf16[256,1024]{1,0:T(8,128)(2,1)}, u32[]{:S(2)}) copy-start(bf16[256,1024]{1,0:T(8,128)(2,1)} %copy-done.8) | copy-start | bytes 1572868
  474.8 45.7 %copy-start.16 = (bf16[1,1,1024,2,352]{2,4,3,1,0:T(8,128)(2,1)S(1)}, bf16[1,1,1024,2,352]{2,4,3,1,0:T(8,128)(2,1)}, u32[]{:S(2)}) copy-start(bf16[1,1,1024,2,352]{2,4,3,1,0:T(8,128)(2,1)} %param.24) | copy-start | bytes 4325380
  525.3 38.2 %all-to-all-start.3 = ((bf16[32,1,20,1024]{3,2,1,0:T(8,128)(2,1)}), bf16[32,1,20,1024]{3,2,1,0:T(8,128)(2,1)S(1)}, u32[]{:S(2)}, u32[]{:S(2)}) async-start(bf16[32,1,20,1024]{3,2,1,0:T(8,128)(2,1)} %copy.64), calls=%async_computation.3 | async-start | bytes 3145728 | tf_op jit(solution)/shard_map/all_to_all | solution.py:140
  531.4 85.8 %all-reduce.11.cloned.1.call-start = ((), (), s32[]{:S(2)}) async-start(), calls=%async_computation.9 | async-start | bytes 1048576 | tf_op jit(solution)/shard_map/psum | solution.py:155
  565.1 52.2 %copy-start.2 = (f32[128,1024]{1,0:T(8,128)S(1)}, f32[128,1024]{1,0:T(8,128)}, u32[]{:S(2)}) copy-start(f32[128,1024]{1,0:T(8,128)} %all-reduce.9.cloned.1.call-done) | copy-start | bytes 1572868
  568.6 53.5 %collective-permute-start.8 = (bf16[1,128,2,256]{1,3,2,0:T(8,128)(2,1)S(1)}, bf16[1,128,2,256]{1,3,2,0:T(8,128)(2,1)S(1)}, u32[]{:S(2)}, u32[]{:S(2)}) collective-permute-start(bf16[1,128,2,256]{1,3,2,0:T(8,128)(2,1)S(1)} %get-tuple-element.462), channel_id=1, source_target_pairs={{128,0},{129,1},{130,2},{131,3},{132,4},{133,5},{134,6},{135,7},{1... | collective-permute-start | bytes 393224 | tf_op jit(solution)/shard_map/ppermute | solution.py:200
  578.5 48.3 %collective-permute-start.6 = (bf16[128,1024]{1,0:T(8,128)(2,1)S(1)}, bf16[128,1024]{1,0:T(8,128)(2,1)S(1)}, u32[]{:S(2)}, u32[]{:S(2)}) collective-permute-start(bf16[128,1024]{1,0:T(8,128)(2,1)S(1)} %get-tuple-element.448), channel_id=1, source_target_pairs={{128,0},{129,1},{130,2},{131,3},{132,4},{133,5},{134,6},{135,7},{1... | collective-permute-start | bytes 786440 | tf_op jit(solution)/shard_map/ppermute | solution.py:199
  617.3 10.4 %copy-start.1 = (s32[2,4096]{1,0:T(2,128)S(1)}, s32[2,4096]{1,0:T(2,128)}, u32[]{:S(2)}) copy-start(s32[2,4096]{1,0:T(2,128)} %param.17) | copy-start | bytes 98308
  618.4 8.3 %collective-permute-start.7 = (bf16[128,1024]{1,0:T(8,128)(2,1)S(1)}, bf16[128,1024]{1,0:T(8,128)(2,1)S(1)}, u32[]{:S(2)}, u32[]{:S(2)}) collective-permute-start(bf16[128,1024]{1,0:T(8,128)(2,1)S(1)} %add_convert_fusion), channel_id=1, source_target_pairs={{0,128},{1,129},{2,130},{3,131},{4,132},{5,133},{6,134},{7,135},{8... | collective-permute-start | bytes 786440 | tf_op jit(solution)/shard_map/ppermute | solution.py:201
  620.8 5.0 collective-permute-start.9
  (6 other events, 19.6 us)
Sparse Core Ops, SparseCore 0:
  18.7 80.6 all-gather.2
  117.8 49.3 all-reduce.4
  270.0 46.9 all-reduce.6
  319.9 84.0 all-gather.4
  422.4 49.3 all-reduce.8
  566.3 50.8 all-reduce.10
where the time goes:
time: 636 us; the launch traced here: 634 us
  waiting for transfers between devices  450 us (71%)
  starting transfers between devices  47.2 us (7%)
  blocking collectives  45.7 us (7%)
  matrix products  30.8 us (5%)
  local copies, waits for them, and re-layouts  23.3 us (4%)
  other arithmetic  22 us (3%)
  between operations  15.4 us (2%)
    all_gather x2, waiting for transfers between devices, one_layer(): piece = lax.all_gather(keys_vals, 'tok', axis=0, tiled=True)  164 us
    psum x2, waiting for transfers between devices, one_layer(): mid = resid + lax.psum(attn_part, 'rep')  98.6 us
    psum x2, waiting for transfers between devices, one_layer(): expert_total = lax.psum(expert_local, 'rep')  84.6 us
    all_to_all x2, waiting for transfers between devices, one_layer(): lax.all_to_all(jnp.einsum('secf,efd->secd', hidden, w_down, preferred_ele...  63.3 us
    all_to_all x1, blocking collectives, one_layer(): lax.all_to_all(copies, 'tok', split_axis=0, concat_axis=0, tiled=True)  45.7 us
    all_to_all x1, waiting for transfers between devices, one_layer(): lax.all_to_all(copies, 'tok', split_axis=0, concat_axis=0, tiled=True)  28.6 us
    all_to_all x2, starting transfers between devices, one_layer(): lax.all_to_all(jnp.einsum('secf,efd->secd', hidden, w_down, preferred_ele...  13.6 us
  transfers between devices with their start and end apart: 19, of which 13 were waited for; matrix products, arithmetic and copies ran while one was open for 4% of the time, Pallas kernels for 0%

commit v1 on v0

--- a/solution.py
+++ b/solution.py
@@ -84,7 +84,9 @@
         jnp.zeros((head_count, tok_rows, HEAD_DIM), jnp.float32),
     )
     empty_pages = jnp.zeros((blocks_dev, PAGE, 2, col_width), jnp.bfloat16)
-    piece = lax.all_gather(keys_vals, "tok", axis=0, tiled=True)
+    piece = jnp.concatenate(
+        lax.all_to_all(jnp.stack([keys_vals] * lax.axis_size("tok")), "tok", 0, 0), axis=0
+    )
     rows_key = piece.shape[0]
     step_rows = 1024
     while rows_key % step_rows != 0:

time: 636 us -> 733 us (1.15)
  local copies, waits for them, and re-layouts: 23.3 us -> 75.7 us
  starting transfers between devices: 47.2 us -> 76.6 us
    all_to_all x0 -> x2, waiting for transfers between devices: none -> 187 us  [one_layer(): lax.all_to_all(jnp.stack([keys_vals] * lax.axis_size('tok')), 'tok', 0, 0)]
    all_gather x2 -> x0, waiting for transfers between devices: 164 us -> none  [one_layer(): piece = lax.all_gather(keys_vals, 'tok', axis=0, tiled=True)]
    while x8 -> x40, local copies, waits for them, and re-layouts: 0.02 us -> 23.8 us
    all_to_all x0 -> x2, starting transfers between devices: none -> 19.6 us  [one_layer(): lax.all_to_all(jnp.stack([keys_vals] * lax.axis_size('tok')), 'tok', 0, 0)]
    slice x8, local copies, waits for them, and re-layouts: 10.2 us -> 26.3 us  [attend(): keys_vals[:, 1].reshape(rows_key, heads_here, head_size).astype(jnp.float32)]
    psum x2, starting transfers between devices: 0.08 us -> 11.6 us  [one_layer(): expert_total = lax.psum(expert_local, 'rep')]
    another operation x2 -> x4, local copies, waits for them, and re-layouts: 0.19 us -> 11.7 us  [the longest x2 11.5 us: one_layer(): jnp.stack([keys_vals] * lax.axis_size('tok'))]
    psum x2, waiting for transfers between devices: 98.6 us -> 91 us  [one_layer(): mid = resid + lax.psum(attn_part, 'rep')]
  transfers between devices with their start and end apart: 19 -> 19, of which waited for: 13 -> 13; matrix products, arithmetic and copies ran while one was open for 4% -> 6% of each run, Pallas kernels for 0% -> 0%
where the time goes in v1:
time: 733 us; the launch traced here: 727 us
  waiting for transfers between devices  455 us (62%)
  starting transfers between devices  76.6 us (10%)
  local copies, waits for them, and re-layouts  75.7 us (10%)
  blocking collectives  45.5 us (6%)
  matrix products  32.4 us (4%)
  other arithmetic  25.4 us (3%)
  between operations  15.4 us (2%)
    all_to_all x2, waiting for transfers between devices, one_layer(): lax.all_to_all(jnp.stack([keys_vals] * lax.axis_size('tok')), 'tok', 0, 0)  187 us
    psum x2, waiting for transfers between devices, one_layer(): mid = resid + lax.psum(attn_part, 'rep')  91 us
    psum x2, waiting for transfers between devices, one_layer(): expert_total = lax.psum(expert_local, 'rep')  82.5 us
    all_to_all x2, waiting for transfers between devices, one_layer(): lax.all_to_all(jnp.einsum('secf,efd->secd', hidden, w_down, preferred_ele...  55.9 us
    all_to_all x1, blocking collectives, one_layer(): lax.all_to_all(copies, 'tok', split_axis=0, concat_axis=0, tiled=True)  45.5 us
    all_to_all x1, waiting for transfers between devices, one_layer(): lax.all_to_all(copies, 'tok', split_axis=0, concat_axis=0, tiled=True)  28.8 us
    slice x8, local copies, waits for them, and re-layouts, attend(): keys_vals[:, 1].reshape(rows_key, heads_here, head_size).astype(jnp.float32)  26.3 us
    while x40, local copies, waits for them, and re-layouts  23.8 us
  transfers between devices with their start and end apart: 19, of which 13 were waited for; matrix products, arithmetic and copies ran while one was open for 6% of the time, Pallas kernels for 0%

profile of v1, /device:TPU:1, one launch (start us, length us, event | category | flops | bytes accessed | tf_op | source)
XLA Modules:
  0.0 726.8 jit_solution(5404764835405888025)
XLA Ops:
  9.0 3.3 collective-permute-start.1
  18.5 5.7 stack.32
  24.2 9.8 %all-to-all-start = ((bf16[32,128,2,256]{3,2,1,0:T(2,128)(2,1)}), bf16[32,128,2,256]{3,2,1,0:T(2,128)(2,1)}, u32[]{:S(2)}, u32[]{:S(2)}) async-start(bf16[32,128,2,256]{3,2,1,0:T(2,128)(2,1)} %stack.32), calls=%async_computation | async-start | bytes 8388608 | tf_op jit(solution)/shard_map/all_to_all | solution.py:88
  36.5 96.9 %all-to-all-done = bf16[32,128,2,256]{3,2,1,0:T(2,128)(2,1)} async-done(((bf16[32,128,2,256]{3,2,1,0:T(2,128)(2,1)}), bf16[32,128,2,256]{3,2,1,0:T(2,128)(2,1)}, u32[]{:S(2)}, u32[]{:S(2)}) %all-to-all-start) | async-done | bytes 4194336 | tf_op jit(solution)/shard_map/all_to_all | solution.py:88
  133.3 35.8 %while.36 = (s32[]{:T(128)}, f32[4,128]{1,0:T(4,128)S(1)}, f32[4,128]{1,0:T(4,128)S(1)}, f32[4,128,64]{1,2,0:T(8,128)S(1)}, s32[128]{0:T(128)S(1)}, /*index=5*/s...) while((s32[]{:T(128)}, f32[4,128]{1,0:T(4,128)S(1)}, ...), condition=%wide.region_4.5_spmd.clone, body=%wide.region_1.4_spmd.clone.sunk | while | flops 476548736 | bytes 12441319 | solution.py:103
  133.7 3.3 constant_dynamic-slice_fusion.9
  142.6 3.4 constant_dynamic-slice_fusion.9
  151.7 3.3 constant_dynamic-slice_fusion.9
  160.6 3.2 constant_dynamic-slice_fusion.9
  171.9 42.2 %all-reduce.5.cloned.1.call-done = f32[128,1024]{1,0:T(8,128)} async-done(((f32[128,1024]{1,0:T(8,128)}), f32[128,1024]{1,0:T(8,128)}) %all-reduce.5.cloned.1.call-update) | async-done | bytes 524304 | tf_op jit(solution)/shard_map/psum | solution.py:113
  218.4 9.7 %all-to-all-start.1 = ((bf16[32,1,20,1024]{3,2,1,0:T(8,128)(2,1)}), bf16[32,1,20,1024]{3,2,1,0:T(8,128)(2,1)S(1)}, u32[]{:S(2)}, u32[]{:S(2)}) async-start(bf16[32,1,20,1024]{3,2,1,0:T(8,128)(2,1)} %bitcast.30), calls=%async_computation.1 | async-start | bytes 3145728 | tf_op jit(solution)/shard_map/all_to_all | solution.py:137
  228.1 3.2 collective-permute-start.5
  234.3 28.8 %all-to-all-done.1 = bf16[32,1,20,1024]{3,2,1,0:T(8,128)(2,1)S(1)} async-done(((bf16[32,1,20,1024]{3,2,1,0:T(8,128)(2,1)}), bf16[32,1,20,1024]{3,2,1,0:T(8,128)(2,1)S(1)}, u32[]{:S(2)}, u32[]{:S(2)}) %all-to-all-start.1) | async-done | bytes 1310752 | tf_op jit(solution)/shard_map/all_to_all | solution.py:137
  270.4 7.5 %all-to-all-start.2 = ((bf16[32,1,20,1024]{3,2,1,0:T(8,128)(2,1)}), bf16[32,1,20,1024]{3,2,1,0:T(8,128)(2,1)S(1)}, u32[]{:S(2)}, u32[]{:S(2)}) async-start(bf16[32,1,20,1024]{3,2,1,0:T(8,128)(2,1)} %copy.67), calls=%async_computation.2 | async-start | bytes 3145728 | tf_op jit(solution)/shard_map/all_to_all | solution.py:142
  277.9 11.4 %all-reduce.7.cloned.1.call-start = ((), (), s32[]{:S(2)}) async-start(), calls=%async_computation.7 | async-start | bytes 1048576 | tf_op jit(solution)/shard_map/psum | solution.py:157
  291.4 24.3 %all-to-all-done.2 = bf16[32,1,20,1024]{3,2,1,0:T(8,128)(2,1)S(1)} async-done(((bf16[32,1,20,1024]{3,2,1,0:T(8,128)(2,1)}), bf16[32,1,20,1024]{3,2,1,0:T(8,128)(2,1)S(1)}, u32[]{:S(2)}, u32[]{:S(2)}) %all-to-all-start.2) | async-done | bytes 1310752 | tf_op jit(solution)/shard_map/all_to_all | solution.py:142
  318.4 45.0 %all-reduce.7.cloned.1.call-done = f32[128,1024]{1,0:T(8,128)} async-done(((f32[128,1024]{1,0:T(8,128)}), f32[128,1024]{1,0:T(8,128)}) %all-reduce.7.cloned.1.call-update) | async-done | bytes 524304 | tf_op jit(solution)/shard_map/psum | solution.py:157
  365.7 5.8 stack.36
  371.5 9.8 %all-to-all-start.3 = ((bf16[32,128,2,256]{3,2,1,0:T(2,128)(2,1)}), bf16[32,128,2,256]{3,2,1,0:T(2,128)(2,1)}, u32[]{:S(2)}, u32[]{:S(2)}) async-start(bf16[32,128,2,256]{3,2,1,0:T(2,128)(2,1)} %stack.36), calls=%async_computation.3 | async-start | bytes 8388608 | tf_op jit(solution)/shard_map/all_to_all | solution.py:88
  381.4 89.7 %all-to-all-done.3 = bf16[32,128,2,256]{3,2,1,0:T(2,128)(2,1)} async-done(((bf16[32,128,2,256]{3,2,1,0:T(2,128)(2,1)}), bf16[32,128,2,256]{3,2,1,0:T(2,128)(2,1)}, u32[]{:S(2)}, u32[]{:S(2)}) %all-to-all-start.3) | async-done | bytes 4194336 | tf_op jit(solution)/shard_map/all_to_all | solution.py:88
  471.1 38.4 %while.37 = (s32[]{:T(128)}, f32[4,128]{1,0:T(4,128)S(1)}, f32[4,128]{1,0:T(4,128)S(1)}, f32[4,128,64]{1,2,0:T(8,128)}, s32[128]{0:T(128)S(1)}, /*index=5*/s32[4...) while((s32[]{:T(128)}, f32[4,128]{1,0:T(4,128)S(1)}, ...), condition=%wide.region_21.23_spmd.clone, body=%wide.region_18.22_spmd.clone.sunk | while | flops 476548736 | bytes 13489951 | solution.py:103
  471.5 3.2 constant_dynamic-slice_fusion.10
  481.0 3.3 constant_dynamic-slice_fusion.10
  490.6 3.4 constant_dynamic-slice_fusion.10
  500.3 3.2 constant_dynamic-slice_fusion.10
  512.6 48.7 %all-reduce.9.cloned.1.call-done = f32[128,1024]{1,0:T(8,128)} async-done(((f32[128,1024]{1,0:T(8,128)}), f32[128,1024]{1,0:T(8,128)}) %all-reduce.9.cloned.1.call-update) | async-done | bytes 524304 | tf_op jit(solution)/shard_map/psum | solution.py:113
  564.3 45.5 %all_to_all.30 = bf16[32,1,20,1024]{3,2,1,0:T(8,128)(2,1)S(1)} all-to-all(bf16[32,1,20,1024]{3,2,1,0:T(8,128)(2,1)S(1)} %bitcast.260), channel_id=1, replica_groups=mesh['section'=2,'tok'=32,'rep'=4] {'tok'}, dimensions={0} | all-to-all | bytes 2621440 | tf_op jit(solution)/shard_map/all_to_all | solution.py:137
  614.7 6.2 all-to-all-start.5
  621.4 31.6 %all-to-all-done.5 = bf16[32,1,20,1024]{3,2,1,0:T(8,128)(2,1)S(1)} async-done(((bf16[32,1,20,1024]{3,2,1,0:T(8,128)(2,1)}), bf16[32,1,20,1024]{3,2,1,0:T(8,128)(2,1)S(1)}, u32[]{:S(2)}, u32[]{:S(2)}) %all-to-all-start.5) | async-done | bytes 1310752 | tf_op jit(solution)/shard_map/all_to_all | solution.py:142
  660.6 9.9 %collective-permute-start.8 = (bf16[1,128,2,256]{3,2,1,0:T(2,128)(2,1)S(1)}, bf16[1,128,2,256]{3,2,1,0:T(2,128)(2,1)S(1)}, u32[]{:S(2)}, u32[]{:S(2)}) collective-permute-start(bf16[1,128,2,256]{3,2,1,0:T(2,128)(2,1)S(1)} %get-tuple-element.510), channel_id=1, source_target_pairs={{128,0},{129,1},{130,2},{131,3},{132,4},{133,5},{134,6},{135,7},{1... | collective-permute-start | bytes 393224 | tf_op jit(solution)/shard_map/ppermute | solution.py:202
  671.8 37.5 %all-reduce.11.cloned.1.call-done = f32[128,1024]{1,0:T(8,128)} async-done(((f32[128,1024]{1,0:T(8,128)}), f32[128,1024]{1,0:T(8,128)}) %all-reduce.11.cloned.1.call-update) | async-done | bytes 524304 | tf_op jit(solution)/shard_map/psum | solution.py:157
  714.1 3.7 collective-permute-done.9
  (273 shorter events, 108.3 us)
Async XLA Ops:
  7.2 29.2 %copy-start = (s32[2,4096]{1,0:T(2,128)S(1)}, s32[2,4096]{1,0:T(2,128)}, u32[]{:S(2)}) copy-start(s32[2,4096]{1,0:T(2,128)} %param.17) | copy-start | bytes 98308
  9.0 7.1 collective-permute-start.1
  12.3 3.2 collective-permute-start
  24.2 109.1 %all-to-all-start = ((bf16[32,128,2,256]{3,2,1,0:T(2,128)(2,1)}), bf16[32,128,2,256]{3,2,1,0:T(2,128)(2,1)}, u32[]{:S(2)}, u32[]{:S(2)}) async-start(bf16[32,128,2,256]{3,2,1,0:T(2,128)(2,1)} %stack.32), calls=%async_computation | async-start | bytes 8388608 | tf_op jit(solution)/shard_map/all_to_all | solution.py:88
  34.0 180.1 %all-reduce.5.cloned.1.call-start = ((), (), s32[]{:S(2)}) async-start(), calls=%async_computation.6 | async-start | bytes 1048576 | tf_op jit(solution)/shard_map/psum | solution.py:113
  34.1 135.2 %collective-permute-start.2 = (bf16[256,1024]{1,0:T(8,128)(2,1)}, bf16[256,1024]{1,0:T(8,128)(2,1)}, u32[]{:S(2)}, u32[]{:S(2)}) collective-permute-start(bf16[256,1024]{1,0:T(8,128)(2,1)} %bitcast.12), channel_id=1, source_target_pairs={{0,128},{128,0},{1,129},{129,1},{2,130},{130,2},{3,131},{131,3},{4... | collective-permute-start | bytes 1572872 | tf_op jit(solution)/shard_map/ppermute | solution.py:186
  169.2 46.2 %copy-start.14 = (f32[1,1024]{1,0:T(1,128)S(1)}, f32[1,1024]{1,0:T(1,128)}, u32[]{:S(2)}) copy-start(f32[1,1024]{1,0:T(1,128)} %get-tuple-element.520) | copy-start | bytes 12292
  218.4 44.8 %all-to-all-start.1 = ((bf16[32,1,20,1024]{3,2,1,0:T(8,128)(2,1)}), bf16[32,1,20,1024]{3,2,1,0:T(8,128)(2,1)S(1)}, u32[]{:S(2)}, u32[]{:S(2)}) async-start(bf16[32,1,20,1024]{3,2,1,0:T(8,128)(2,1)} %bitcast.30), calls=%async_computation.1 | async-start | bytes 3145728 | tf_op jit(solution)/shard_map/all_to_all | solution.py:137
  228.1 6.2 collective-permute-start.5
  231.3 35.0 %collective-permute-start.4 = (bf16[1,352,1024]{2,1,0:T(8,128)(2,1)}, bf16[1,352,1024]{2,1,0:T(8,128)(2,1)}, u32[]{:S(2)}, u32[]{:S(2)}) collective-permute-start(bf16[1,352,1024]{2,1,0:T(8,128)(2,1)} %bitcast.287), channel_id=1, source_target_pairs={{0,128},{128,0},{1,129},{129,1},{2,130},{130,2},{3,131},{131,3},{4... | collective-permute-start | bytes 2162696 | tf_op jit(solution)/shard_map/ppermute | solution.py:186
  270.4 20.9 %copy-start.15 = (s32[128,2]{0,1:T(2,128)S(1)}, s32[128,2]{0,1:T(2,128)}, u32[]{:S(2)}) copy-start(s32[128,2]{0,1:T(2,128)} %get-tuple-element.517) | copy-start | bytes 3076
  270.4 45.3 %all-to-all-start.2 = ((bf16[32,1,20,1024]{3,2,1,0:T(8,128)(2,1)}), bf16[32,1,20,1024]{3,2,1,0:T(8,128)(2,1)S(1)}, u32[]{:S(2)}, u32[]{:S(2)}) async-start(bf16[32,1,20,1024]{3,2,1,0:T(8,128)(2,1)} %copy.67), calls=%async_computation.2 | async-start | bytes 3145728 | tf_op jit(solution)/shard_map/all_to_all | solution.py:142
  277.9 85.6 %all-reduce.7.cloned.1.call-start = ((), (), s32[]{:S(2)}) async-start(), calls=%async_computation.7 | async-start | bytes 1048576 | tf_op jit(solution)/shard_map/psum | solution.py:157
  289.3 1.8 collective-permute-start.3
  290.3 27.0 %copy-start.20 = (pred[256]{0:T(512)(128)(4,1)}, pred[256]{0:T(512)(128)(4,1)S(1)}, u32[]{:S(2)}) copy-start(pred[256]{0:T(512)(128)(4,1)S(1)} %get-tuple-element.497) | copy-start | bytes 772
  317.3 46.2 %copy-start.3 = (f32[128,1024]{1,0:T(8,128)S(1)}, f32[128,1024]{1,0:T(8,128)}, u32[]{:S(2)}) copy-start(f32[128,1024]{1,0:T(8,128)} %all-reduce.5.cloned.1.call-done) | copy-start | bytes 1572868
  317.3 46.1 %copy-start.5 = (bf16[2,128,1024]{2,1,0:T(8,128)(2,1)S(1)}, bf16[2,128,1024]{2,1,0:T(8,128)(2,1)}, u32[]{:S(2)}) copy-start(bf16[2,128,1024]{2,1,0:T(8,128)(2,1)} %param.16) | copy-start | bytes 1572868
  317.5 47.2 %copy-start.7 = (bf16[1,1024,3,256]{1,3,2,0:T(8,128)(2,1)S(1)}, bf16[1,1024,3,256]{1,3,2,0:T(8,128)(2,1)}, u32[]{:S(2)}) copy-start(bf16[1,1024,3,256]{1,3,2,0:T(8,128)(2,1)} %copy-done.6) | copy-start | bytes 4718596
  317.5 47.2 %copy-start.22 = (f32[1,1024]{1,0:T(1,128)S(1)}, f32[1,1024]{1,0:T(1,128)}, u32[]{:S(2)}) copy-start(f32[1,1024]{1,0:T(1,128)} %get-tuple-element.513) | copy-start | bytes 12292
  371.5 99.6 %copy-start.12 = (s32[128]{0:T(128)S(1)}, s32[128]{0:T(128)}, u32[]{:S(2)}) copy-start(s32[128]{0:T(128)} %copy-done.11) | copy-start | bytes 1540
  371.5 99.6 %all-to-all-start.3 = ((bf16[32,128,2,256]{3,2,1,0:T(2,128)(2,1)}), bf16[32,128,2,256]{3,2,1,0:T(2,128)(2,1)}, u32[]{:S(2)}, u32[]{:S(2)}) async-start(bf16[32,128,2,256]{3,2,1,0:T(2,128)(2,1)} %stack.36), calls=%async_computation.3 | async-start | bytes 8388608 | tf_op jit(solution)/shard_map/all_to_all | solution.py:88
  381.3 180.0 %all-reduce.9.cloned.1.call-start = ((), (), s32[]{:S(2)}) async-start(), calls=%async_computation.8 | async-start | bytes 1048576 | tf_op jit(solution)/shard_map/psum | solution.py:113
  509.5 53.0 %copy-start.13 = (f32[1,1024]{1,0:T(1,128)S(1)}, f32[1,1024]{1,0:T(1,128)}, u32[]{:S(2)}) copy-start(f32[1,1024]{1,0:T(1,128)} %get-tuple-element.514) | copy-start | bytes 12292
  564.3 45.6 %copy-start.26 = (bf16[1,1,1024,2,352]{2,4,3,1,0:T(8,128)(2,1)S(1)}, bf16[1,1,1024,2,352]{2,4,3,1,0:T(8,128)(2,1)}, u32[]{:S(2)}) copy-start(bf16[1,1,1024,2,352]{2,4,3,1,0:T(8,128)(2,1)} %param.24) | copy-start | bytes 4325380
  614.7 38.3 %all-to-all-start.5 = ((bf16[32,1,20,1024]{3,2,1,0:T(8,128)(2,1)}), bf16[32,1,20,1024]{3,2,1,0:T(8,128)(2,1)S(1)}, u32[]{:S(2)}, u32[]{:S(2)}) async-start(bf16[32,1,20,1024]{3,2,1,0:T(8,128)(2,1)} %copy.74), calls=%async_computation.5 | async-start | bytes 3145728 | tf_op jit(solution)/shard_map/all_to_all | solution.py:142
  620.9 88.4 %all-reduce.11.cloned.1.call-start = ((), (), s32[]{:S(2)}) async-start(), calls=%async_computation.9 | async-start | bytes 1048576 | tf_op jit(solution)/shard_map/psum | solution.py:157
  657.2 52.2 %copy-start.2 = (f32[128,1024]{1,0:T(8,128)S(1)}, f32[128,1024]{1,0:T(8,128)}, u32[]{:S(2)}) copy-start(f32[128,1024]{1,0:T(8,128)} %all-reduce.9.cloned.1.call-done) | copy-start | bytes 1572868
  660.6 59.4 %copy-start.1 = (s32[2,4096]{1,0:T(2,128)S(1)}, s32[2,4096]{1,0:T(2,128)}, u32[]{:S(2)}) copy-start(s32[2,4096]{1,0:T(2,128)} %param.17) | copy-start | bytes 98308
  660.6 53.5 %collective-permute-start.8 = (bf16[1,128,2,256]{3,2,1,0:T(2,128)(2,1)S(1)}, bf16[1,128,2,256]{3,2,1,0:T(2,128)(2,1)S(1)}, u32[]{:S(2)}, u32[]{:S(2)}) collective-permute-start(bf16[1,128,2,256]{3,2,1,0:T(2,128)(2,1)S(1)} %get-tuple-element.510), channel_id=1, source_target_pairs={{128,0},{129,1},{130,2},{131,3},{132,4},{133,5},{134,6},{135,7},{1... | collective-permute-start | bytes 393224 | tf_op jit(solution)/shard_map/ppermute | solution.py:202
  670.5 48.7 %collective-permute-start.6 = (bf16[128,1024]{1,0:T(8,128)(2,1)S(1)}, bf16[128,1024]{1,0:T(8,128)(2,1)S(1)}, u32[]{:S(2)}, u32[]{:S(2)}) collective-permute-start(bf16[128,1024]{1,0:T(8,128)(2,1)S(1)} %get-tuple-element.496), channel_id=1, source_target_pairs={{128,0},{129,1},{130,2},{131,3},{132,4},{133,5},{134,6},{135,7},{1... | collective-permute-start | bytes 786440 | tf_op jit(solution)/shard_map/ppermute | solution.py:201
  710.5 8.7 %collective-permute-start.7 = (bf16[128,1024]{1,0:T(8,128)(2,1)S(1)}, bf16[128,1024]{1,0:T(8,128)(2,1)S(1)}, u32[]{:S(2)}, u32[]{:S(2)}) collective-permute-start(bf16[128,1024]{1,0:T(8,128)(2,1)S(1)} %add_convert_fusion), channel_id=1, source_target_pairs={{0,128},{1,129},{2,130},{3,131},{4,132},{5,133},{6,134},{7,135},{8... | collective-permute-start | bytes 786440 | tf_op jit(solution)/shard_map/ppermute | solution.py:203
  712.8 5.0 collective-permute-start.9
  (22 other events, 81.6 us)
Sparse Core Ops, SparseCore 0:
  171.7 42.4 all-reduce.4
  318.6 44.8 all-reduce.6
  512.7 48.5 all-reduce.8
  658.4 50.8 all-reduce.10
